TPU v7x, 512 devices: a whole 4x4x16 slice. The times are simulated.
512 devices in a mesh: gx: 32 (over z_hi, x, core), gy: 4 (over y), gz: 4 (over z_lo).
Axes of the slice: x: 4, y: 4, z: 16 (z_hi: 4, z_lo: 4; z = z_hi * 4 + z_lo), core: 2. Of those that a mesh axis runs over, the one named last changes fastest.
Arguments:
- level_set: float32 [1024, 128, 512], P('gx', 'gy', 'gz'), may hold values from -6 to 6
- velocity: bfloat16 [3, 1024, 128, 512], P(None, 'gx', 'gy', 'gz'), may hold values from -1 to 1
- active_brick: int32 [32, 4, 4], P('gx', 'gy', 'gz'), may hold values 0 or 1
- depth_order: int32 [4], replicated, may hold values from 0 to 3, as said below
Outputs:
- level_out: float32 [1024, 128, 512], P('gx', 'gy', 'gz')
- image: float32 [4, 2048, 256], P(None, ('gx', 'gz'), 'gy')
Inputs may be any that keep to these rules, and one draw needn't show every extreme that they name: `depth_order`: either 0, 1, .. in slab order or the reverse.
All inputs are finite; a program needn't handle non-finite values. No bound on the sum of `active_brick` on one device may be relied on, other than what follows from the above.
Results may differ from a plain program's by a relative error of at most 0.0003.
Values may be sent and summed in bfloat16 or wider, within the bound.
No kernel may reach another device: no remote copies, remote signals or barrier semaphores. Data moves between devices by JAX's collectives and lax.ppermute only.
A program may use at most 64 MiB of HBM per device.

v0:
```python
import jax
import jax.numpy as jnp
from jax import lax
from jax.sharding import PartitionSpec as P

CZ = 128
time_step = 0.4
weno_floor = 1e-06


def extended(x, sides, width):
    for axis, dim in sides:
        size, length = (lax.axis_size(axis), x.shape[dim])
        up = [(i, (i + 1) % size) for i in range(size)]
        down = [(j, i) for i, j in up]
        last = lax.slice_in_dim(x, length - width, length, axis=dim)
        initial = lax.slice_in_dim(x, 0, width, axis=dim)
        before = lax.ppermute(last, axis, up)
        after = lax.ppermute(initial, axis, down)
        x = jnp.concatenate([before, x, after], axis=dim)
    return x


def square(operand):
    return operand * operand


def weno_value(diff_one, diff_two, diff_three, diff_four, diff_five):
    candidate_one = diff_one / 3.0 - 7.0 * diff_two / 6.0 + 11.0 * diff_three / 6.0
    candidate_two = -diff_two / 6.0 + 5.0 * diff_three / 6.0 + diff_four / 3.0
    candidate_three = diff_three / 3.0 + 5.0 * diff_four / 6.0 - diff_five / 6.0
    smooth_one = 13.0 / 12.0 * square(diff_one - 2.0 * diff_two + diff_three) + 0.25 * square(
        diff_one - 4.0 * diff_two + 3.0 * diff_three
    )
    smooth_two = 13.0 / 12.0 * square(diff_two - 2.0 * diff_three + diff_four) + 0.25 * square(
        diff_two - diff_four
    )
    smooth_three = 13.0 / 12.0 * square(diff_three - 2.0 * diff_four + diff_five) + 0.25 * square(
        3.0 * diff_three - 4.0 * diff_four + diff_five
    )
    weight_one = 0.1 / square(weno_floor + smooth_one)
    weight_two = 0.6 / square(weno_floor + smooth_two)
    weight_three = 0.3 / square(weno_floor + smooth_three)
    return (
        weight_one * candidate_one + weight_two * candidate_two + weight_three * candidate_three
    ) / (weight_one + weight_two + weight_three)


def window(padded, axis_dim, offset):
    slicing = [slice(3, extent - 3) for extent in padded.shape]
    length = padded.shape[axis_dim] - 6
    slicing[axis_dim] = slice(3 + offset, 3 + offset + length)
    return padded[tuple(slicing)]


def local_rate(padded, velocity_window):
    summed = jnp.zeros(velocity_window.shape[1:], jnp.float32)
    for axis_dim in range(3):
        jump_list = [
            window(padded, axis_dim, offset) - window(padded, axis_dim, offset - 1)
            for offset in range(-2, 4)
        ]
        from_left = weno_value(jump_list[0], jump_list[1], jump_list[2], jump_list[3], jump_list[4])
        from_right = weno_value(
            jump_list[5], jump_list[4], jump_list[3], jump_list[2], jump_list[1]
        )
        speed_axis = velocity_window[axis_dim].astype(jnp.float32)
        summed = (
            summed
            + jnp.maximum(speed_axis, 0.0) * from_left
            + jnp.minimum(speed_axis, 0.0) * from_right
        )
    return -summed


def shade(samples, alive, ascending):
    opacity = alive * (2.0 / CZ) / (1.0 + 4.0 * samples * samples)
    log_clear = jnp.log1p(-opacity)
    depth = jnp.arange(CZ)
    ahead = jnp.where(
        ascending, depth[:, None] < depth[None, :], depth[:, None] > depth[None, :]
    ).astype(jnp.float32)
    flat_logs = log_clear.reshape(-1, CZ)
    before = jnp.dot(flat_logs, ahead, precision=lax.Precision.HIGHEST).reshape(log_clear.shape)
    weight = jnp.exp(before) * opacity
    bright = jnp.tanh(samples)
    red = jnp.sum(weight * (0.5 + 0.5 * bright), -1)
    green = jnp.sum(weight * (0.5 - 0.5 * bright), -1)
    blue = jnp.sum(weight / (1.0 + samples * samples), -1)
    clear = jnp.exp(jnp.sum(log_clear, -1))
    return jnp.stack([red, green, blue, clear])


def alternate(grid_pairs):
    row_list = [jnp.stack(pixel_pair, -1) for pixel_pair in grid_pairs]
    joined = jnp.stack(row_list, -3)
    joined_shape = joined.shape
    return joined.reshape(joined_shape[:-4] + (joined_shape[-4] * 2, joined_shape[-2] * 2))


def over(front_part, back_part):
    colour = front_part[:3] + front_part[3:] * back_part[:3]
    clear = front_part[3:] * back_part[3:]
    return jnp.concatenate([colour, clear], 0)


def shards(level_set, velocity, active_brick, depth_order):

    def section_rate(level_field):
        padded = extended(level_field, (("gx", 0), ("gy", 1), ("gz", 2)), 3)
        return local_rate(padded, velocity)

    section_one = level_set + time_step * section_rate(level_set)
    section_two = 0.75 * level_set + 0.25 * (section_one + time_step * section_rate(section_one))
    advanced = level_set / 3.0 + 2.0 / 3.0 * (section_two + time_step * section_rate(section_two))
    alive = active_brick[0, 0, 0] > 0
    level_out = jnp.where(alive, advanced, level_set)
    alive_float = alive.astype(jnp.float32)
    group = lax.axis_size("gz")
    ascending = depth_order[0] < depth_order[group - 1]
    rim = extended(level_out.astype(jnp.bfloat16), (("gx", 0), ("gy", 1)), 1).astype(
        level_out.dtype
    )
    left_x = 0.75 * rim[1:-1] + 0.25 * rim[:-2]
    right_x = 0.75 * rim[1:-1] + 0.25 * rim[2:]
    grid_pairs = []
    for along_x in (left_x, right_x):
        pair_list = []
        for neighbour in (along_x[:, :-2], along_x[:, 2:]):
            samples = 0.75 * along_x[:, 1:-1] + 0.25 * neighbour
            pair_list.append(shade(samples, alive_float, ascending))
        grid_pairs.append(pair_list)
    slab_image = alternate(grid_pairs)
    rows_each = slab_image.shape[1] // group
    columns = slab_image.shape[2]
    pieces = slab_image.reshape(4, group, rows_each, columns)
    received = lax.all_to_all(pieces, "gz", split_axis=1, concat_axis=1, tiled=True)
    blended = jnp.concatenate(
        [
            jnp.zeros((3, rows_each, columns), jnp.float32),
            jnp.ones((1, rows_each, columns), jnp.float32),
        ],
        0,
    )
    for rank_value in range(group):
        chooser = (depth_order == rank_value).astype(jnp.float32)
        piece_now = jnp.einsum("s,csij->cij", chooser, received, precision=lax.Precision.HIGHEST)
        blended = over(blended, piece_now)
    image = jnp.concatenate([blended[:3], 1.0 - blended[3:]], 0)
    return (level_out, image)


def solution(mesh):
    placed = (P("gx", "gy", "gz"), P(None, "gx", "gy", "gz"), P("gx", "gy", "gz"), P())
    return jax.shard_map(
        shards,
        mesh=mesh,
        in_specs=placed,
        out_specs=(P("gx", "gy", "gz"), P(None, ("gx", "gz"), "gy")),
        check_vma=False,
    )
```

profile of v0, /device:TPU:32, one launch (start us, length us, event | category | flops | bytes accessed | tf_op | source)
XLA Modules:
  0.0 195.8 jit_solution(901559053685275974)
XLA Ops:
  3.4 13.5 %collective-permute-start.1 = (f32[3,32,128]{2,1,0:T(8,128)S(1)}, f32[3,32,128]{2,1,0:T(8,128)S(1)}, u32[]{:S(2)}, u32[]{:S(2)}) collective-permute-start(f32[3,32,128]{2,1,0:T(8,128)S(1)} %get-tuple-element.55), channel_id=1, source_target_pairs={{16,0},{32,16},{48,32},{64,48},{80,64},{96,80},{112,96},{128,112},... | collective-permute-start | bytes 147464 | tf_op jit(solution)/shard_map/ppermute | solution.py:19
  18.6 4.9 %collective-permute-start.3 = (f32[38,3,128]{2,1,0:T(4,128)S(1)}, f32[38,3,128]{2,1,0:T(4,128)S(1)}, u32[]{:S(2)}, u32[]{:S(2)}) collective-permute-start(f32[38,3,128]{2,1,0:T(4,128)S(1)} %get-tuple-element.47), channel_id=1, source_target_pairs={{4,0},{8,4},{12,8},{0,12},{5,1},{9,5},{13,9},{1,13},{6,2},{10,6},{... | collective-permute-start | bytes 175112 | tf_op jit(solution)/shard_map/ppermute | solution.py:19
  25.6 5.5 %collective-permute-done.2 = f32[38,3,128]{2,1,0:T(4,128)S(1)} collective-permute-done((f32[38,3,128]{2,1,0:T(4,128)S(1)}, f32[38,3,128]{2,1,0:T(4,128)S(1)}, u32[]{:S(2)}, u32[]{:S(2)}) %collective-permute-start.2) | collective-permute-done | bytes 58400 | tf_op jit(solution)/shard_map/ppermute | solution.py:18
  32.4 2.9 %collective-permute-start.4 = (f32[38,38,3]{1,0,2:T(8,128)}, f32[38,38,3]{1,0,2:T(8,128)S(1)}, u32[]{:S(2)}, u32[]{:S(2)}) collective-permute-start(f32[38,38,3]{1,0,2:T(8,128)} %copy.7), channel_id=1, source_target_pairs={{0,1},{1,2},{2,3},{3,0},{4,5},{5,6},{6,7},{7,4},{8,9},{9,10},{10,1... | collective-permute-start | bytes 51992 | tf_op jit(solution)/shard_map/ppermute | solution.py:18
  35.7 2.9 %collective-permute-start.5 = (f32[38,38,3]{1,0,2:T(8,128)S(1)}, f32[38,38,3]{1,0,2:T(8,128)S(1)}, u32[]{:S(2)}, u32[]{:S(2)}) collective-permute-start(f32[38,38,3]{1,0,2:T(8,128)S(1)} %copy.9), channel_id=1, source_target_pairs={{1,0},{2,1},{3,2},{0,3},{5,4},{6,5},{7,6},{4,7},{9,8},{10,9},{11,1... | collective-permute-start | bytes 51992 | tf_op jit(solution)/shard_map/ppermute | solution.py:19
  39.1 2.7 %collective-permute-done.5 = f32[38,38,3]{1,0,2:T(8,128)S(1)} collective-permute-done((f32[38,38,3]{1,0,2:T(8,128)S(1)}, f32[38,38,3]{1,0,2:T(8,128)S(1)}, u32[]{:S(2)}, u32[]{:S(2)}) %collective-permute-start.5) | collective-permute-done | bytes 17360 | tf_op jit(solution)/shard_map/ppermute | solution.py:19
  45.1 8.4 %fusion.27 = f32[32,32,128]{2,1,0:T(8,128)S(1)} fusion(f32[32,32,128]{2,1,0:T(8,128)S(1)} %copy-done, f32[38,38,131]{2,1,0:T(8,128)S(1)} %get-tuple-element.29, f32[38,38,131]{2,1,0:T(8,128)S(1)} %get-tuple-element.28, f32[38,3,128]{2,1,0:T(4,128)S(1)} %collective-permute-done.3, f32[38,32,128]{2,1,0:T(8,128)S(1)} %get-tuple-element.67, ...), kind=kLoop, calls=%fused_computation.81 | loop fusion | flops 54919168 | bytes 8865792 | tf_op jit(solution)/shard_map/add | solution.py:113
  53.5 7.0 %collective-permute-start.7 = (f32[3,32,128]{2,1,0:T(8,128)S(1)}, f32[3,32,128]{2,1,0:T(8,128)S(1)}, u32[]{:S(2)}, u32[]{:S(2)}) collective-permute-start(f32[3,32,128]{2,1,0:T(8,128)S(1)} %get-tuple-element.51), channel_id=1, source_target_pairs={{16,0},{32,16},{48,32},{64,48},{80,64},{96,80},{112,96},{128,112},... | collective-permute-start | bytes 147464 | tf_op jit(solution)/shard_map/ppermute | solution.py:19
  62.4 9.7 %collective-permute-done.6 = f32[3,32,128]{2,1,0:T(8,128)S(1)} collective-permute-done((f32[3,32,128]{2,1,0:T(8,128)S(1)}, f32[3,32,128]{2,1,0:T(8,128)S(1)}, u32[]{:S(2)}, u32[]{:S(2)}) %collective-permute-start.6) | collective-permute-done | bytes 49184 | tf_op jit(solution)/shard_map/ppermute | solution.py:18
  74.1 3.9 %collective-permute-start.8 = (f32[38,3,128]{2,1,0:T(4,128)S(1)}, f32[38,3,128]{2,1,0:T(4,128)S(1)}, u32[]{:S(2)}, u32[]{:S(2)}) collective-permute-start(f32[38,3,128]{2,1,0:T(4,128)S(1)} %get-tuple-element.44), channel_id=1, source_target_pairs={{0,4},{4,8},{8,12},{12,0},{1,5},{5,9},{9,13},{13,1},{2,6},{6,10},{... | collective-permute-start | bytes 175112 | tf_op jit(solution)/shard_map/ppermute | solution.py:18
  78.5 3.1 %collective-permute-done.8 = f32[38,3,128]{2,1,0:T(4,128)S(1)} collective-permute-done((f32[38,3,128]{2,1,0:T(4,128)S(1)}, f32[38,3,128]{2,1,0:T(4,128)S(1)}, u32[]{:S(2)}, u32[]{:S(2)}) %collective-permute-start.8) | collective-permute-done | bytes 58400 | tf_op jit(solution)/shard_map/ppermute | solution.py:18
  82.3 3.4 %collective-permute-start.10 = (f32[38,38,3]{1,0,2:T(8,128)S(1)}, f32[38,38,3]{1,0,2:T(8,128)S(1)}, u32[]{:S(2)}, u32[]{:S(2)}) collective-permute-start(f32[38,38,3]{1,0,2:T(8,128)S(1)} %copy.11), channel_id=1, source_target_pairs={{0,1},{1,2},{2,3},{3,0},{4,5},{5,6},{6,7},{7,4},{8,9},{9,10},{10,1... | collective-permute-start | bytes 51992 | tf_op jit(solution)/shard_map/ppermute | solution.py:18
  86.1 2.4 %collective-permute-start.11 = (f32[38,38,3]{1,0,2:T(8,128)S(1)}, f32[38,38,3]{1,0,2:T(8,128)S(1)}, u32[]{:S(2)}, u32[]{:S(2)}) collective-permute-start(f32[38,38,3]{1,0,2:T(8,128)S(1)} %copy.13), channel_id=1, source_target_pairs={{1,0},{2,1},{3,2},{0,3},{5,4},{6,5},{7,6},{4,7},{9,8},{10,9},{11,1... | collective-permute-start | bytes 51992 | tf_op jit(solution)/shard_map/ppermute | solution.py:19
  90.0 3.1 %collective-permute-done.11 = f32[38,38,3]{1,0,2:T(8,128)S(1)} collective-permute-done((f32[38,38,3]{1,0,2:T(8,128)S(1)}, f32[38,38,3]{1,0,2:T(8,128)S(1)}, u32[]{:S(2)}, u32[]{:S(2)}) %collective-permute-start.11) | collective-permute-done | bytes 17360 | tf_op jit(solution)/shard_map/ppermute | solution.py:19
  96.6 8.6 %fusion.37 = f32[32,32,128]{2,1,0:T(8,128)S(1)} fusion(f32[32,32,128]{2,1,0:T(8,128)S(1)} %fusion.27, f32[38,38,131]{2,1,0:T(8,128)S(1)} %get-tuple-element.25, f32[38,38,131]{2,1,0:T(8,128)S(1)} %get-tuple-element.24, f32[38,35,128]{2,1,0:T(8,128)S(1)} %get-tuple-element.43, f32[38,35,128]{2,1,0:T(8,128)S(1)} %get-tuple-element.42, ...), kind=kLoop, calls=%fused_computation.91 | loop fusion | flops 55312384 | bytes 8749056 | tf_op jit(solution)/shard_map/add | solution.py:114
  109.5 9.6 %collective-permute-done.12 = f32[3,32,128]{2,1,0:T(8,128)S(1)} collective-permute-done((f32[3,32,128]{2,1,0:T(8,128)S(1)}, f32[3,32,128]{2,1,0:T(8,128)S(1)}, u32[]{:S(2)}, u32[]{:S(2)}) %collective-permute-start.12) | collective-permute-done | bytes 49184 | tf_op jit(solution)/shard_map/ppermute | solution.py:18
  121.1 3.9 %collective-permute-start.14 = (f32[38,3,128]{2,1,0:T(4,128)S(1)}, f32[38,3,128]{2,1,0:T(4,128)S(1)}, u32[]{:S(2)}, u32[]{:S(2)}) collective-permute-start(f32[38,3,128]{2,1,0:T(4,128)S(1)} %get-tuple-element.40), channel_id=1, source_target_pairs={{0,4},{4,8},{8,12},{12,0},{1,5},{5,9},{9,13},{13,1},{2,6},{6,10},{... | collective-permute-start | bytes 175112 | tf_op jit(solution)/shard_map/ppermute | solution.py:18
  125.7 2.9 %collective-permute-done.14 = f32[38,3,128]{2,1,0:T(4,128)S(1)} collective-permute-done((f32[38,3,128]{2,1,0:T(4,128)S(1)}, f32[38,3,128]{2,1,0:T(4,128)S(1)}, u32[]{:S(2)}, u32[]{:S(2)}) %collective-permute-start.14) | collective-permute-done | bytes 58400 | tf_op jit(solution)/shard_map/ppermute | solution.py:18
  129.3 3.9 %collective-permute-start.16 = (f32[38,38,3]{1,0,2:T(8,128)S(1)}, f32[38,38,3]{1,0,2:T(8,128)S(1)}, u32[]{:S(2)}, u32[]{:S(2)}) collective-permute-start(f32[38,38,3]{1,0,2:T(8,128)S(1)} %copy.15), channel_id=1, source_target_pairs={{0,1},{1,2},{2,3},{3,0},{4,5},{5,6},{6,7},{7,4},{8,9},{9,10},{10,1... | collective-permute-start | bytes 51992 | tf_op jit(solution)/shard_map/ppermute | solution.py:18
  137.1 2.6 %collective-permute-done.17 = f32[38,38,3]{1,0,2:T(8,128)S(1)} collective-permute-done((f32[38,38,3]{1,0,2:T(8,128)S(1)}, f32[38,38,3]{1,0,2:T(8,128)S(1)}, u32[]{:S(2)}, u32[]{:S(2)}) %collective-permute-start.17) | collective-permute-done | bytes 17360 | tf_op jit(solution)/shard_map/ppermute | solution.py:19
  143.2 9.4 %fusion.219 = (bf16[32,32,128]{2,1,0:T(8,128)(2,1)S(1)}, f32[32,32,128]{2,1,0:T(8,128)}) fusion(f32[32,32,128]{2,1,0:T(8,128)S(1)} %copy-done, f32[32,32,128]{2,1,0:T(8,128)S(1)} %fusion.37, f32[38,38,131]{2,1,0:T(8,128)S(1)} %get-tuple-element.21, f32[38,38,131]{2,1,0:T(8,128)S(1)} %get-tuple-element.20, bf16[3,32,32,128]{3,2,1,0:T(8,128)(2,1)S(1)} %copy-done.3, ...), kind=kLoop, calls=%fused_computation.358 | loop fusion | flops 55574528 | bytes 9011201 | tf_op jit(solution)/shard_map/convert_element_type | solution.py:121
  156.9 8.6 %collective-permute-done.18 = bf16[1,32,128]{2,1,0:T(8,128)(2,1)S(1)} collective-permute-done((bf16[1,32,128]{2,1,0:T(8,128)(2,1)S(1)}, bf16[1,32,128]{2,1,0:T(8,128)(2,1)S(1)}, u32[]{:S(2)}, u32[]{:S(2)}) %collective-permute-start.18) | collective-permute-done | bytes 8224 | tf_op jit(solution)/shard_map/ppermute | solution.py:18
  167.7 3.6 %collective-permute-start.20 = (bf16[34,1,128]{2,1,0:T(2,128)(2,1)S(1)}, bf16[34,1,128]{2,1,0:T(2,128)(2,1)S(1)}, u32[]{:S(2)}, u32[]{:S(2)}) collective-permute-start(bf16[34,1,128]{2,1,0:T(2,128)(2,1)S(1)} %get-tuple-element.57), channel_id=1, source_target_pairs={{0,4},{4,8},{8,12},{12,0},{1,5},{5,9},{9,13},{13,1},{2,6},{6,10},{... | collective-permute-start | bytes 26120 | tf_op jit(solution)/shard_map/ppermute | solution.py:18
  182.1 10.3 %all_to_all.5 = f32[4,1,4096]{2,1,0:T(1,128)S(1)} all-to-all(f32[4,1,4096]{2,1,0:T(1,128)S(1)} %reshape.79), channel_id=1, replica_groups=mesh['gx'=32,'gy'=4,'gz'=4] {'gz'}, dimensions={0} | all-to-all | bytes 131072 | tf_op jit(solution)/shard_map/all_to_all | solution.py:137
  (100 shorter events, 55.9 us)
Async XLA Ops:
  1.5 15.4 %collective-permute-start = (f32[3,32,128]{2,1,0:T(8,128)S(1)}, f32[3,32,128]{2,1,0:T(8,128)S(1)}, u32[]{:S(2)}, u32[]{:S(2)}) collective-permute-start(f32[3,32,128]{2,1,0:T(8,128)S(1)} %get-tuple-element.56), channel_id=1, source_target_pairs={{0,16},{16,32},{32,48},{48,64},{64,80},{80,96},{96,112},{112,128},... | collective-permute-start | bytes 147464 | tf_op jit(solution)/shard_map/ppermute | solution.py:18
  3.4 15.2 %collective-permute-start.1 = (f32[3,32,128]{2,1,0:T(8,128)S(1)}, f32[3,32,128]{2,1,0:T(8,128)S(1)}, u32[]{:S(2)}, u32[]{:S(2)}) collective-permute-start(f32[3,32,128]{2,1,0:T(8,128)S(1)} %get-tuple-element.55), channel_id=1, source_target_pairs={{16,0},{32,16},{48,32},{64,48},{80,64},{96,80},{112,96},{128,112},... | collective-permute-start | bytes 147464 | tf_op jit(solution)/shard_map/ppermute | solution.py:19
  18.6 6.9 %collective-permute-start.3 = (f32[38,3,128]{2,1,0:T(4,128)S(1)}, f32[38,3,128]{2,1,0:T(4,128)S(1)}, u32[]{:S(2)}, u32[]{:S(2)}) collective-permute-start(f32[38,3,128]{2,1,0:T(4,128)S(1)} %get-tuple-element.47), channel_id=1, source_target_pairs={{4,0},{8,4},{12,8},{0,12},{5,1},{9,5},{13,9},{1,13},{6,2},{10,6},{... | collective-permute-start | bytes 175112 | tf_op jit(solution)/shard_map/ppermute | solution.py:19
  23.6 7.5 %collective-permute-start.2 = (f32[38,3,128]{2,1,0:T(4,128)S(1)}, f32[38,3,128]{2,1,0:T(4,128)S(1)}, u32[]{:S(2)}, u32[]{:S(2)}) collective-permute-start(f32[38,3,128]{2,1,0:T(4,128)S(1)} %get-tuple-element.46), channel_id=1, source_target_pairs={{0,4},{4,8},{8,12},{12,0},{1,5},{5,9},{9,13},{13,1},{2,6},{6,10},{... | collective-permute-start | bytes 175112 | tf_op jit(solution)/shard_map/ppermute | solution.py:18
  32.4 6.3 %collective-permute-start.4 = (f32[38,38,3]{1,0,2:T(8,128)}, f32[38,38,3]{1,0,2:T(8,128)S(1)}, u32[]{:S(2)}, u32[]{:S(2)}) collective-permute-start(f32[38,38,3]{1,0,2:T(8,128)} %copy.7), channel_id=1, source_target_pairs={{0,1},{1,2},{2,3},{3,0},{4,5},{5,6},{6,7},{7,4},{8,9},{9,10},{10,1... | collective-permute-start | bytes 51992 | tf_op jit(solution)/shard_map/ppermute | solution.py:18
  35.7 6.1 %collective-permute-start.5 = (f32[38,38,3]{1,0,2:T(8,128)S(1)}, f32[38,38,3]{1,0,2:T(8,128)S(1)}, u32[]{:S(2)}, u32[]{:S(2)}) collective-permute-start(f32[38,38,3]{1,0,2:T(8,128)S(1)} %copy.9), channel_id=1, source_target_pairs={{1,0},{2,1},{3,2},{0,3},{5,4},{6,5},{7,6},{4,7},{9,8},{10,9},{11,1... | collective-permute-start | bytes 51992 | tf_op jit(solution)/shard_map/ppermute | solution.py:19
  53.5 8.9 %collective-permute-start.7 = (f32[3,32,128]{2,1,0:T(8,128)S(1)}, f32[3,32,128]{2,1,0:T(8,128)S(1)}, u32[]{:S(2)}, u32[]{:S(2)}) collective-permute-start(f32[3,32,128]{2,1,0:T(8,128)S(1)} %get-tuple-element.51), channel_id=1, source_target_pairs={{16,0},{32,16},{48,32},{64,48},{80,64},{96,80},{112,96},{128,112},... | collective-permute-start | bytes 147464 | tf_op jit(solution)/shard_map/ppermute | solution.py:19
  60.5 11.6 %collective-permute-start.6 = (f32[3,32,128]{2,1,0:T(8,128)S(1)}, f32[3,32,128]{2,1,0:T(8,128)S(1)}, u32[]{:S(2)}, u32[]{:S(2)}) collective-permute-start(f32[3,32,128]{2,1,0:T(8,128)S(1)} %get-tuple-element.50), channel_id=1, source_target_pairs={{0,16},{16,32},{32,48},{48,64},{64,80},{80,96},{96,112},{112,128},... | collective-permute-start | bytes 147464 | tf_op jit(solution)/shard_map/ppermute | solution.py:18
  72.2 6.3 %collective-permute-start.9 = (f32[38,3,128]{2,1,0:T(4,128)S(1)}, f32[38,3,128]{2,1,0:T(4,128)S(1)}, u32[]{:S(2)}, u32[]{:S(2)}) collective-permute-start(f32[38,3,128]{2,1,0:T(4,128)S(1)} %get-tuple-element.45), channel_id=1, source_target_pairs={{4,0},{8,4},{12,8},{0,12},{5,1},{9,5},{13,9},{1,13},{6,2},{10,6},{... | collective-permute-start | bytes 175112 | tf_op jit(solution)/shard_map/ppermute | solution.py:19
  74.1 7.5 %collective-permute-start.8 = (f32[38,3,128]{2,1,0:T(4,128)S(1)}, f32[38,3,128]{2,1,0:T(4,128)S(1)}, u32[]{:S(2)}, u32[]{:S(2)}) collective-permute-start(f32[38,3,128]{2,1,0:T(4,128)S(1)} %get-tuple-element.44), channel_id=1, source_target_pairs={{0,4},{4,8},{8,12},{12,0},{1,5},{5,9},{9,13},{13,1},{2,6},{6,10},{... | collective-permute-start | bytes 175112 | tf_op jit(solution)/shard_map/ppermute | solution.py:18
  82.3 6.4 %collective-permute-start.10 = (f32[38,38,3]{1,0,2:T(8,128)S(1)}, f32[38,38,3]{1,0,2:T(8,128)S(1)}, u32[]{:S(2)}, u32[]{:S(2)}) collective-permute-start(f32[38,38,3]{1,0,2:T(8,128)S(1)} %copy.11), channel_id=1, source_target_pairs={{0,1},{1,2},{2,3},{3,0},{4,5},{5,6},{6,7},{7,4},{8,9},{9,10},{10,1... | collective-permute-start | bytes 51992 | tf_op jit(solution)/shard_map/ppermute | solution.py:18
  86.1 7.0 %collective-permute-start.11 = (f32[38,38,3]{1,0,2:T(8,128)S(1)}, f32[38,38,3]{1,0,2:T(8,128)S(1)}, u32[]{:S(2)}, u32[]{:S(2)}) collective-permute-start(f32[38,38,3]{1,0,2:T(8,128)S(1)} %copy.13), channel_id=1, source_target_pairs={{1,0},{2,1},{3,2},{0,3},{5,4},{6,5},{7,6},{4,7},{9,8},{10,9},{11,1... | collective-permute-start | bytes 51992 | tf_op jit(solution)/shard_map/ppermute | solution.py:19
  94.4 2.2 %copy-start.2 = (bf16[3,32,32,128]{3,2,1,0:T(8,128)(2,1)S(1)}, bf16[3,32,32,128]{3,2,1,0:T(8,128)(2,1)}, u32[]{:S(2)}) copy-start(bf16[3,32,32,128]{3,2,1,0:T(8,128)(2,1)} %param.5) | copy-start | bytes 2359300
  105.2 4.3 %collective-permute-start.13 = (f32[3,32,128]{2,1,0:T(8,128)S(1)}, f32[3,32,128]{2,1,0:T(8,128)S(1)}, u32[]{:S(2)}, u32[]{:S(2)}) collective-permute-start(f32[3,32,128]{2,1,0:T(8,128)S(1)} %get-tuple-element.49), channel_id=1, source_target_pairs={{16,0},{32,16},{48,32},{64,48},{80,64},{96,80},{112,96},{128,112},... | collective-permute-start | bytes 147464 | tf_op jit(solution)/shard_map/ppermute | solution.py:19
  107.1 12.0 %collective-permute-start.12 = (f32[3,32,128]{2,1,0:T(8,128)S(1)}, f32[3,32,128]{2,1,0:T(8,128)S(1)}, u32[]{:S(2)}, u32[]{:S(2)}) collective-permute-start(f32[3,32,128]{2,1,0:T(8,128)S(1)} %get-tuple-element.48), channel_id=1, source_target_pairs={{0,16},{16,32},{32,48},{48,64},{64,80},{80,96},{96,112},{112,128},... | collective-permute-start | bytes 147464 | tf_op jit(solution)/shard_map/ppermute | solution.py:18
  119.1 6.5 %collective-permute-start.15 = (f32[38,3,128]{2,1,0:T(4,128)S(1)}, f32[38,3,128]{2,1,0:T(4,128)S(1)}, u32[]{:S(2)}, u32[]{:S(2)}) collective-permute-start(f32[38,3,128]{2,1,0:T(4,128)S(1)} %get-tuple-element.41), channel_id=1, source_target_pairs={{4,0},{8,4},{12,8},{0,12},{5,1},{9,5},{13,9},{1,13},{6,2},{10,6},{... | collective-permute-start | bytes 175112 | tf_op jit(solution)/shard_map/ppermute | solution.py:19
  121.1 7.5 %collective-permute-start.14 = (f32[38,3,128]{2,1,0:T(4,128)S(1)}, f32[38,3,128]{2,1,0:T(4,128)S(1)}, u32[]{:S(2)}, u32[]{:S(2)}) collective-permute-start(f32[38,3,128]{2,1,0:T(4,128)S(1)} %get-tuple-element.40), channel_id=1, source_target_pairs={{0,4},{4,8},{8,12},{12,0},{1,5},{5,9},{9,13},{13,1},{2,6},{6,10},{... | collective-permute-start | bytes 175112 | tf_op jit(solution)/shard_map/ppermute | solution.py:18
  129.3 6.5 %collective-permute-start.16 = (f32[38,38,3]{1,0,2:T(8,128)S(1)}, f32[38,38,3]{1,0,2:T(8,128)S(1)}, u32[]{:S(2)}, u32[]{:S(2)}) collective-permute-start(f32[38,38,3]{1,0,2:T(8,128)S(1)} %copy.15), channel_id=1, source_target_pairs={{0,1},{1,2},{2,3},{3,0},{4,5},{5,6},{6,7},{7,4},{8,9},{9,10},{10,1... | collective-permute-start | bytes 51992 | tf_op jit(solution)/shard_map/ppermute | solution.py:18
  133.6 6.1 %collective-permute-start.17 = (f32[38,38,3]{1,0,2:T(8,128)S(1)}, f32[38,38,3]{1,0,2:T(8,128)S(1)}, u32[]{:S(2)}, u32[]{:S(2)}) collective-permute-start(f32[38,38,3]{1,0,2:T(8,128)S(1)} %copy.17), channel_id=1, source_target_pairs={{1,0},{2,1},{3,2},{0,3},{5,4},{6,5},{7,6},{4,7},{9,8},{10,9},{11,1... | collective-permute-start | bytes 51992 | tf_op jit(solution)/shard_map/ppermute | solution.py:19
  143.2 28.2 %copy-start.4 = (s32[4]{0:T(128)S(1)}, s32[4]{0:T(128)}, u32[]{:S(2)}) copy-start(s32[4]{0:T(128)} %param.7) | copy-start | bytes 52
  152.5 4.3 %collective-permute-start.19 = (bf16[1,32,128]{2,1,0:T(8,128)(2,1)S(1)}, bf16[1,32,128]{2,1,0:T(8,128)(2,1)S(1)}, u32[]{:S(2)}, u32[]{:S(2)}) collective-permute-start(bf16[1,32,128]{2,1,0:T(8,128)(2,1)S(1)} %get-tuple-element.60), channel_id=1, source_target_pairs={{16,0},{32,16},{48,32},{64,48},{80,64},{96,80},{112,96},{128,112},... | collective-permute-start | bytes 24584 | tf_op jit(solution)/shard_map/ppermute | solution.py:19
  154.5 11.0 %collective-permute-start.18 = (bf16[1,32,128]{2,1,0:T(8,128)(2,1)S(1)}, bf16[1,32,128]{2,1,0:T(8,128)(2,1)S(1)}, u32[]{:S(2)}, u32[]{:S(2)}) collective-permute-start(bf16[1,32,128]{2,1,0:T(8,128)(2,1)S(1)} %get-tuple-element.59), channel_id=1, source_target_pairs={{0,16},{16,32},{32,48},{48,64},{64,80},{80,96},{96,112},{112,128},... | collective-permute-start | bytes 24584 | tf_op jit(solution)/shard_map/ppermute | solution.py:18
  165.5 7.6 %collective-permute-start.21 = (bf16[34,1,128]{2,1,0:T(2,128)(2,1)S(1)}, bf16[34,1,128]{2,1,0:T(2,128)(2,1)S(1)}, u32[]{:S(2)}, u32[]{:S(2)}) collective-permute-start(bf16[34,1,128]{2,1,0:T(2,128)(2,1)S(1)} %get-tuple-element.58), channel_id=1, source_target_pairs={{4,0},{8,4},{12,8},{0,12},{5,1},{9,5},{13,9},{1,13},{6,2},{10,6},{... | collective-permute-start | bytes 26120 | tf_op jit(solution)/shard_map/ppermute | solution.py:19
  167.7 6.9 %collective-permute-start.20 = (bf16[34,1,128]{2,1,0:T(2,128)(2,1)S(1)}, bf16[34,1,128]{2,1,0:T(2,128)(2,1)S(1)}, u32[]{:S(2)}, u32[]{:S(2)}) collective-permute-start(bf16[34,1,128]{2,1,0:T(2,128)(2,1)S(1)} %get-tuple-element.57), channel_id=1, source_target_pairs={{0,4},{4,8},{8,12},{12,0},{1,5},{5,9},{9,13},{13,1},{2,6},{6,10},{... | collective-permute-start | bytes 26120 | tf_op jit(solution)/shard_map/ppermute | solution.py:18
  (3 other events, 6.1 us)
where the time goes:
time: 197 us; the launch traced here: 196 us
  starting transfers between devices  75 us (38%)
  waiting for transfers between devices  50.3 us (26%)
  other arithmetic  35.4 us (18%)
  local copies, waits for them, and re-layouts  15.9 us (8%)
  blocking collectives  10.3 us (5%)
  matrix products  5.91 us (3%)
  between operations  3.05 us (2%)
    ppermute x11, starting transfers between devices, extended(): after = lax.ppermute(initial, axis, down)  42.7 us
    ppermute x11, waiting for transfers between devices, extended(): before = lax.ppermute(last, axis, up)  40.9 us
    ppermute x11, starting transfers between devices, extended(): before = lax.ppermute(last, axis, up)  32.3 us
    all_to_all x1, blocking collectives, shards(): lax.all_to_all(pieces, 'gz', split_axis=1, concat_axis=1, tiled=True)  10.3 us
    ppermute x11, waiting for transfers between devices, extended(): after = lax.ppermute(initial, axis, down)  9.37 us
    convert_element_type x1, other arithmetic, shards(): level_out.astype(jnp.bfloat16)  9.35 us
    add x1, other arithmetic, shards(): 0.75 * level_set  8.59 us
    add x1, other arithmetic, shards(): section_one = level_set + time_step * section_rate(level_set)  8.38 us
  transfers between devices with their start and end apart: 22, of which 14 were waited for; matrix products, arithmetic and copies ran while one was open for 3% of the time, Pallas kernels for 0%

commit v1 on v0

--- a/solution.py
+++ b/solution.py
@@ -134,7 +134,10 @@
     rows_each = slab_image.shape[1] // group
     columns = slab_image.shape[2]
     pieces = slab_image.reshape(4, group, rows_each, columns)
-    received = lax.all_to_all(pieces, "gz", split_axis=1, concat_axis=1, tiled=True)
+    received = jnp.concatenate(
+        lax.all_to_all(jnp.stack(jnp.split(pieces, lax.axis_size("gz"), axis=1)), "gz", 0, 0),
+        axis=1,
+    )
     blended = jnp.concatenate(
         [
             jnp.zeros((3, rows_each, columns), jnp.float32),

time: 197 us -> 200 us (1.015)
  local copies, waits for them, and re-layouts: 15.9 us -> 19.3 us
    another operation x1 -> x5, local copies, waits for them, and re-layouts: 0.68 us -> 4.12 us  [shards(): jnp.stack(jnp.split(pieces, lax.axis_size('gz'), axis=1))]
where the time goes in v1:
time: 200 us; the launch traced here: 199 us
  starting transfers between devices  75 us (38%)
  waiting for transfers between devices  50.2 us (25%)
  other arithmetic  35.4 us (18%)
  local copies, waits for them, and re-layouts  19.3 us (10%)
  blocking collectives  10.3 us (5%)
  matrix products  5.92 us (3%)
  between operations  3.13 us (2%)
    ppermute x11, starting transfers between devices, extended(): after = lax.ppermute(initial, axis, down)  42.7 us
    ppermute x11, waiting for transfers between devices, extended(): before = lax.ppermute(last, axis, up)  40.8 us
    ppermute x11, starting transfers between devices, extended(): before = lax.ppermute(last, axis, up)  32.3 us
    all_to_all x1, blocking collectives, shards(): lax.all_to_all(jnp.stack(jnp.split(pieces, lax.axis_size('gz'), axis=1)),...  10.3 us
    ppermute x11, waiting for transfers between devices, extended(): after = lax.ppermute(initial, axis, down)  9.39 us
    convert_element_type x1, other arithmetic, shards(): level_out.astype(jnp.bfloat16)  9.35 us
    add x1, other arithmetic, shards(): 0.75 * level_set  8.59 us
    add x1, other arithmetic, shards(): section_one = level_set + time_step * section_rate(level_set)  8.38 us
  transfers between devices with their start and end apart: 22, of which 14 were waited for; matrix products, arithmetic and copies ran while one was open for 3% of the time, Pallas kernels for 0%

profile of v1, /device:TPU:32, one launch (start us, length us, event | category | flops | bytes accessed | tf_op | source)
XLA Modules:
  0.0 199.3 jit_solution(1236003350197501221)
XLA Ops:
  3.4 13.5 %collective-permute-start.1 = (f32[3,32,128]{2,1,0:T(8,128)S(1)}, f32[3,32,128]{2,1,0:T(8,128)S(1)}, u32[]{:S(2)}, u32[]{:S(2)}) collective-permute-start(f32[3,32,128]{2,1,0:T(8,128)S(1)} %get-tuple-element.59), channel_id=1, source_target_pairs={{16,0},{32,16},{48,32},{64,48},{80,64},{96,80},{112,96},{128,112},... | collective-permute-start | bytes 147464 | tf_op jit(solution)/shard_map/ppermute | solution.py:19
  18.6 4.9 %collective-permute-start.3 = (f32[38,3,128]{2,1,0:T(4,128)S(1)}, f32[38,3,128]{2,1,0:T(4,128)S(1)}, u32[]{:S(2)}, u32[]{:S(2)}) collective-permute-start(f32[38,3,128]{2,1,0:T(4,128)S(1)} %get-tuple-element.51), channel_id=1, source_target_pairs={{4,0},{8,4},{12,8},{0,12},{5,1},{9,5},{13,9},{1,13},{6,2},{10,6},{... | collective-permute-start | bytes 175112 | tf_op jit(solution)/shard_map/ppermute | solution.py:19
  25.6 5.5 %collective-permute-done.2 = f32[38,3,128]{2,1,0:T(4,128)S(1)} collective-permute-done((f32[38,3,128]{2,1,0:T(4,128)S(1)}, f32[38,3,128]{2,1,0:T(4,128)S(1)}, u32[]{:S(2)}, u32[]{:S(2)}) %collective-permute-start.2) | collective-permute-done | bytes 58400 | tf_op jit(solution)/shard_map/ppermute | solution.py:18
  32.4 2.9 %collective-permute-start.4 = (f32[38,38,3]{1,0,2:T(8,128)}, f32[38,38,3]{1,0,2:T(8,128)S(1)}, u32[]{:S(2)}, u32[]{:S(2)}) collective-permute-start(f32[38,38,3]{1,0,2:T(8,128)} %copy.10), channel_id=1, source_target_pairs={{0,1},{1,2},{2,3},{3,0},{4,5},{5,6},{6,7},{7,4},{8,9},{9,10},{10,1... | collective-permute-start | bytes 51992 | tf_op jit(solution)/shard_map/ppermute | solution.py:18
  35.7 2.9 %collective-permute-start.5 = (f32[38,38,3]{1,0,2:T(8,128)S(1)}, f32[38,38,3]{1,0,2:T(8,128)S(1)}, u32[]{:S(2)}, u32[]{:S(2)}) collective-permute-start(f32[38,38,3]{1,0,2:T(8,128)S(1)} %copy.12), channel_id=1, source_target_pairs={{1,0},{2,1},{3,2},{0,3},{5,4},{6,5},{7,6},{4,7},{9,8},{10,9},{11,1... | collective-permute-start | bytes 51992 | tf_op jit(solution)/shard_map/ppermute | solution.py:19
  39.1 2.7 %collective-permute-done.5 = f32[38,38,3]{1,0,2:T(8,128)S(1)} collective-permute-done((f32[38,38,3]{1,0,2:T(8,128)S(1)}, f32[38,38,3]{1,0,2:T(8,128)S(1)}, u32[]{:S(2)}, u32[]{:S(2)}) %collective-permute-start.5) | collective-permute-done | bytes 17360 | tf_op jit(solution)/shard_map/ppermute | solution.py:19
  45.1 8.4 %fusion.27 = f32[32,32,128]{2,1,0:T(8,128)S(1)} fusion(f32[32,32,128]{2,1,0:T(8,128)S(1)} %copy-done, f32[38,38,131]{2,1,0:T(8,128)S(1)} %get-tuple-element.33, f32[38,38,131]{2,1,0:T(8,128)S(1)} %get-tuple-element.32, f32[38,3,128]{2,1,0:T(4,128)S(1)} %collective-permute-done.3, f32[38,32,128]{2,1,0:T(8,128)S(1)} %get-tuple-element.71, ...), kind=kLoop, calls=%fused_computation.81 | loop fusion | flops 54919168 | bytes 8865792 | tf_op jit(solution)/shard_map/add | solution.py:113
  53.5 7.0 %collective-permute-start.7 = (f32[3,32,128]{2,1,0:T(8,128)S(1)}, f32[3,32,128]{2,1,0:T(8,128)S(1)}, u32[]{:S(2)}, u32[]{:S(2)}) collective-permute-start(f32[3,32,128]{2,1,0:T(8,128)S(1)} %get-tuple-element.55), channel_id=1, source_target_pairs={{16,0},{32,16},{48,32},{64,48},{80,64},{96,80},{112,96},{128,112},... | collective-permute-start | bytes 147464 | tf_op jit(solution)/shard_map/ppermute | solution.py:19
  62.4 9.7 %collective-permute-done.6 = f32[3,32,128]{2,1,0:T(8,128)S(1)} collective-permute-done((f32[3,32,128]{2,1,0:T(8,128)S(1)}, f32[3,32,128]{2,1,0:T(8,128)S(1)}, u32[]{:S(2)}, u32[]{:S(2)}) %collective-permute-start.6) | collective-permute-done | bytes 49184 | tf_op jit(solution)/shard_map/ppermute | solution.py:18
  74.1 3.9 %collective-permute-start.8 = (f32[38,3,128]{2,1,0:T(4,128)S(1)}, f32[38,3,128]{2,1,0:T(4,128)S(1)}, u32[]{:S(2)}, u32[]{:S(2)}) collective-permute-start(f32[38,3,128]{2,1,0:T(4,128)S(1)} %get-tuple-element.48), channel_id=1, source_target_pairs={{0,4},{4,8},{8,12},{12,0},{1,5},{5,9},{9,13},{13,1},{2,6},{6,10},{... | collective-permute-start | bytes 175112 | tf_op jit(solution)/shard_map/ppermute | solution.py:18
  78.4 3.1 %collective-permute-done.8 = f32[38,3,128]{2,1,0:T(4,128)S(1)} collective-permute-done((f32[38,3,128]{2,1,0:T(4,128)S(1)}, f32[38,3,128]{2,1,0:T(4,128)S(1)}, u32[]{:S(2)}, u32[]{:S(2)}) %collective-permute-start.8) | collective-permute-done | bytes 58400 | tf_op jit(solution)/shard_map/ppermute | solution.py:18
  82.3 3.4 %collective-permute-start.10 = (f32[38,38,3]{1,0,2:T(8,128)S(1)}, f32[38,38,3]{1,0,2:T(8,128)S(1)}, u32[]{:S(2)}, u32[]{:S(2)}) collective-permute-start(f32[38,38,3]{1,0,2:T(8,128)S(1)} %copy.14), channel_id=1, source_target_pairs={{0,1},{1,2},{2,3},{3,0},{4,5},{5,6},{6,7},{7,4},{8,9},{9,10},{10,1... | collective-permute-start | bytes 51992 | tf_op jit(solution)/shard_map/ppermute | solution.py:18
  86.1 2.4 %collective-permute-start.11 = (f32[38,38,3]{1,0,2:T(8,128)S(1)}, f32[38,38,3]{1,0,2:T(8,128)S(1)}, u32[]{:S(2)}, u32[]{:S(2)}) collective-permute-start(f32[38,38,3]{1,0,2:T(8,128)S(1)} %copy.16), channel_id=1, source_target_pairs={{1,0},{2,1},{3,2},{0,3},{5,4},{6,5},{7,6},{4,7},{9,8},{10,9},{11,1... | collective-permute-start | bytes 51992 | tf_op jit(solution)/shard_map/ppermute | solution.py:19
  90.0 3.1 %collective-permute-done.11 = f32[38,38,3]{1,0,2:T(8,128)S(1)} collective-permute-done((f32[38,38,3]{1,0,2:T(8,128)S(1)}, f32[38,38,3]{1,0,2:T(8,128)S(1)}, u32[]{:S(2)}, u32[]{:S(2)}) %collective-permute-start.11) | collective-permute-done | bytes 17360 | tf_op jit(solution)/shard_map/ppermute | solution.py:19
  96.6 8.6 %fusion.37 = f32[32,32,128]{2,1,0:T(8,128)S(1)} fusion(f32[32,32,128]{2,1,0:T(8,128)S(1)} %fusion.27, f32[38,38,131]{2,1,0:T(8,128)S(1)} %get-tuple-element.29, f32[38,38,131]{2,1,0:T(8,128)S(1)} %get-tuple-element.28, f32[38,35,128]{2,1,0:T(8,128)S(1)} %get-tuple-element.47, f32[38,35,128]{2,1,0:T(8,128)S(1)} %get-tuple-element.46, ...), kind=kLoop, calls=%fused_computation.91 | loop fusion | flops 55312384 | bytes 8749056 | tf_op jit(solution)/shard_map/add | solution.py:114
  109.5 9.6 %collective-permute-done.12 = f32[3,32,128]{2,1,0:T(8,128)S(1)} collective-permute-done((f32[3,32,128]{2,1,0:T(8,128)S(1)}, f32[3,32,128]{2,1,0:T(8,128)S(1)}, u32[]{:S(2)}, u32[]{:S(2)}) %collective-permute-start.12) | collective-permute-done | bytes 49184 | tf_op jit(solution)/shard_map/ppermute | solution.py:18
  121.1 3.9 %collective-permute-start.14 = (f32[38,3,128]{2,1,0:T(4,128)S(1)}, f32[38,3,128]{2,1,0:T(4,128)S(1)}, u32[]{:S(2)}, u32[]{:S(2)}) collective-permute-start(f32[38,3,128]{2,1,0:T(4,128)S(1)} %get-tuple-element.44), channel_id=1, source_target_pairs={{0,4},{4,8},{8,12},{12,0},{1,5},{5,9},{9,13},{13,1},{2,6},{6,10},{... | collective-permute-start | bytes 175112 | tf_op jit(solution)/shard_map/ppermute | solution.py:18
  125.7 2.9 %collective-permute-done.14 = f32[38,3,128]{2,1,0:T(4,128)S(1)} collective-permute-done((f32[38,3,128]{2,1,0:T(4,128)S(1)}, f32[38,3,128]{2,1,0:T(4,128)S(1)}, u32[]{:S(2)}, u32[]{:S(2)}) %collective-permute-start.14) | collective-permute-done | bytes 58400 | tf_op jit(solution)/shard_map/ppermute | solution.py:18
  129.3 3.9 %collective-permute-start.16 = (f32[38,38,3]{1,0,2:T(8,128)S(1)}, f32[38,38,3]{1,0,2:T(8,128)S(1)}, u32[]{:S(2)}, u32[]{:S(2)}) collective-permute-start(f32[38,38,3]{1,0,2:T(8,128)S(1)} %copy.18), channel_id=1, source_target_pairs={{0,1},{1,2},{2,3},{3,0},{4,5},{5,6},{6,7},{7,4},{8,9},{9,10},{10,1... | collective-permute-start | bytes 51992 | tf_op jit(solution)/shard_map/ppermute | solution.py:18
  137.1 2.6 %collective-permute-done.17 = f32[38,38,3]{1,0,2:T(8,128)S(1)} collective-permute-done((f32[38,38,3]{1,0,2:T(8,128)S(1)}, f32[38,38,3]{1,0,2:T(8,128)S(1)}, u32[]{:S(2)}, u32[]{:S(2)}) %collective-permute-start.17) | collective-permute-done | bytes 17360 | tf_op jit(solution)/shard_map/ppermute | solution.py:19
  143.2 9.4 %fusion.219 = (bf16[32,32,128]{2,1,0:T(8,128)(2,1)S(1)}, f32[32,32,128]{2,1,0:T(8,128)}) fusion(f32[32,32,128]{2,1,0:T(8,128)S(1)} %copy-done, f32[32,32,128]{2,1,0:T(8,128)S(1)} %fusion.37, f32[38,38,131]{2,1,0:T(8,128)S(1)} %get-tuple-element.25, f32[38,38,131]{2,1,0:T(8,128)S(1)} %get-tuple-element.24, bf16[3,32,32,128]{3,2,1,0:T(8,128)(2,1)S(1)} %copy-done.3, ...), kind=kLoop, calls=%fused_computation.363 | loop fusion | flops 55574528 | bytes 9011201 | tf_op jit(solution)/shard_map/convert_element_type | solution.py:121
  156.9 8.6 %collective-permute-done.18 = bf16[1,32,128]{2,1,0:T(8,128)(2,1)S(1)} collective-permute-done((bf16[1,32,128]{2,1,0:T(8,128)(2,1)S(1)}, bf16[1,32,128]{2,1,0:T(8,128)(2,1)S(1)}, u32[]{:S(2)}, u32[]{:S(2)}) %collective-permute-start.18) | collective-permute-done | bytes 8224 | tf_op jit(solution)/shard_map/ppermute | solution.py:18
  167.7 3.6 %collective-permute-start.20 = (bf16[34,1,128]{2,1,0:T(2,128)(2,1)S(1)}, bf16[34,1,128]{2,1,0:T(2,128)(2,1)S(1)}, u32[]{:S(2)}, u32[]{:S(2)}) collective-permute-start(bf16[34,1,128]{2,1,0:T(2,128)(2,1)S(1)} %get-tuple-element.61), channel_id=1, source_target_pairs={{0,4},{4,8},{8,12},{12,0},{1,5},{5,9},{9,13},{13,1},{2,6},{6,10},{... | collective-permute-start | bytes 26120 | tf_op jit(solution)/shard_map/ppermute | solution.py:18
  185.6 10.3 %all_to_all.5 = f32[4,1,4096]{2,1,0:T(1,128)S(1)} all-to-all(f32[4,1,4096]{2,1,0:T(1,128)S(1)} %reshape.87), channel_id=1, replica_groups=mesh['gx'=32,'gy'=4,'gz'=4] {'gz'}, dimensions={0} | all-to-all | bytes 131072 | tf_op jit(solution)/shard_map/all_to_all | solution.py:138
  (105 shorter events, 59.3 us)
Async XLA Ops:
  1.5 15.4 %collective-permute-start = (f32[3,32,128]{2,1,0:T(8,128)S(1)}, f32[3,32,128]{2,1,0:T(8,128)S(1)}, u32[]{:S(2)}, u32[]{:S(2)}) collective-permute-start(f32[3,32,128]{2,1,0:T(8,128)S(1)} %get-tuple-element.60), channel_id=1, source_target_pairs={{0,16},{16,32},{32,48},{48,64},{64,80},{80,96},{96,112},{112,128},... | collective-permute-start | bytes 147464 | tf_op jit(solution)/shard_map/ppermute | solution.py:18
  3.4 15.2 %collective-permute-start.1 = (f32[3,32,128]{2,1,0:T(8,128)S(1)}, f32[3,32,128]{2,1,0:T(8,128)S(1)}, u32[]{:S(2)}, u32[]{:S(2)}) collective-permute-start(f32[3,32,128]{2,1,0:T(8,128)S(1)} %get-tuple-element.59), channel_id=1, source_target_pairs={{16,0},{32,16},{48,32},{64,48},{80,64},{96,80},{112,96},{128,112},... | collective-permute-start | bytes 147464 | tf_op jit(solution)/shard_map/ppermute | solution.py:19
  18.6 6.9 %collective-permute-start.3 = (f32[38,3,128]{2,1,0:T(4,128)S(1)}, f32[38,3,128]{2,1,0:T(4,128)S(1)}, u32[]{:S(2)}, u32[]{:S(2)}) collective-permute-start(f32[38,3,128]{2,1,0:T(4,128)S(1)} %get-tuple-element.51), channel_id=1, source_target_pairs={{4,0},{8,4},{12,8},{0,12},{5,1},{9,5},{13,9},{1,13},{6,2},{10,6},{... | collective-permute-start | bytes 175112 | tf_op jit(solution)/shard_map/ppermute | solution.py:19
  23.6 7.5 %collective-permute-start.2 = (f32[38,3,128]{2,1,0:T(4,128)S(1)}, f32[38,3,128]{2,1,0:T(4,128)S(1)}, u32[]{:S(2)}, u32[]{:S(2)}) collective-permute-start(f32[38,3,128]{2,1,0:T(4,128)S(1)} %get-tuple-element.50), channel_id=1, source_target_pairs={{0,4},{4,8},{8,12},{12,0},{1,5},{5,9},{9,13},{13,1},{2,6},{6,10},{... | collective-permute-start | bytes 175112 | tf_op jit(solution)/shard_map/ppermute | solution.py:18
  32.4 6.3 %collective-permute-start.4 = (f32[38,38,3]{1,0,2:T(8,128)}, f32[38,38,3]{1,0,2:T(8,128)S(1)}, u32[]{:S(2)}, u32[]{:S(2)}) collective-permute-start(f32[38,38,3]{1,0,2:T(8,128)} %copy.10), channel_id=1, source_target_pairs={{0,1},{1,2},{2,3},{3,0},{4,5},{5,6},{6,7},{7,4},{8,9},{9,10},{10,1... | collective-permute-start | bytes 51992 | tf_op jit(solution)/shard_map/ppermute | solution.py:18
  35.7 6.1 %collective-permute-start.5 = (f32[38,38,3]{1,0,2:T(8,128)S(1)}, f32[38,38,3]{1,0,2:T(8,128)S(1)}, u32[]{:S(2)}, u32[]{:S(2)}) collective-permute-start(f32[38,38,3]{1,0,2:T(8,128)S(1)} %copy.12), channel_id=1, source_target_pairs={{1,0},{2,1},{3,2},{0,3},{5,4},{6,5},{7,6},{4,7},{9,8},{10,9},{11,1... | collective-permute-start | bytes 51992 | tf_op jit(solution)/shard_map/ppermute | solution.py:19
  53.5 8.9 %collective-permute-start.7 = (f32[3,32,128]{2,1,0:T(8,128)S(1)}, f32[3,32,128]{2,1,0:T(8,128)S(1)}, u32[]{:S(2)}, u32[]{:S(2)}) collective-permute-start(f32[3,32,128]{2,1,0:T(8,128)S(1)} %get-tuple-element.55), channel_id=1, source_target_pairs={{16,0},{32,16},{48,32},{64,48},{80,64},{96,80},{112,96},{128,112},... | collective-permute-start | bytes 147464 | tf_op jit(solution)/shard_map/ppermute | solution.py:19
  60.5 11.6 %collective-permute-start.6 = (f32[3,32,128]{2,1,0:T(8,128)S(1)}, f32[3,32,128]{2,1,0:T(8,128)S(1)}, u32[]{:S(2)}, u32[]{:S(2)}) collective-permute-start(f32[3,32,128]{2,1,0:T(8,128)S(1)} %get-tuple-element.54), channel_id=1, source_target_pairs={{0,16},{16,32},{32,48},{48,64},{64,80},{80,96},{96,112},{112,128},... | collective-permute-start | bytes 147464 | tf_op jit(solution)/shard_map/ppermute | solution.py:18
  72.2 6.3 %collective-permute-start.9 = (f32[38,3,128]{2,1,0:T(4,128)S(1)}, f32[38,3,128]{2,1,0:T(4,128)S(1)}, u32[]{:S(2)}, u32[]{:S(2)}) collective-permute-start(f32[38,3,128]{2,1,0:T(4,128)S(1)} %get-tuple-element.49), channel_id=1, source_target_pairs={{4,0},{8,4},{12,8},{0,12},{5,1},{9,5},{13,9},{1,13},{6,2},{10,6},{... | collective-permute-start | bytes 175112 | tf_op jit(solution)/shard_map/ppermute | solution.py:19
  74.1 7.5 %collective-permute-start.8 = (f32[38,3,128]{2,1,0:T(4,128)S(1)}, f32[38,3,128]{2,1,0:T(4,128)S(1)}, u32[]{:S(2)}, u32[]{:S(2)}) collective-permute-start(f32[38,3,128]{2,1,0:T(4,128)S(1)} %get-tuple-element.48), channel_id=1, source_target_pairs={{0,4},{4,8},{8,12},{12,0},{1,5},{5,9},{9,13},{13,1},{2,6},{6,10},{... | collective-permute-start | bytes 175112 | tf_op jit(solution)/shard_map/ppermute | solution.py:18
  82.3 6.4 %collective-permute-start.10 = (f32[38,38,3]{1,0,2:T(8,128)S(1)}, f32[38,38,3]{1,0,2:T(8,128)S(1)}, u32[]{:S(2)}, u32[]{:S(2)}) collective-permute-start(f32[38,38,3]{1,0,2:T(8,128)S(1)} %copy.14), channel_id=1, source_target_pairs={{0,1},{1,2},{2,3},{3,0},{4,5},{5,6},{6,7},{7,4},{8,9},{9,10},{10,1... | collective-permute-start | bytes 51992 | tf_op jit(solution)/shard_map/ppermute | solution.py:18
  86.1 7.0 %collective-permute-start.11 = (f32[38,38,3]{1,0,2:T(8,128)S(1)}, f32[38,38,3]{1,0,2:T(8,128)S(1)}, u32[]{:S(2)}, u32[]{:S(2)}) collective-permute-start(f32[38,38,3]{1,0,2:T(8,128)S(1)} %copy.16), channel_id=1, source_target_pairs={{1,0},{2,1},{3,2},{0,3},{5,4},{6,5},{7,6},{4,7},{9,8},{10,9},{11,1... | collective-permute-start | bytes 51992 | tf_op jit(solution)/shard_map/ppermute | solution.py:19
  105.2 4.3 %collective-permute-start.13 = (f32[3,32,128]{2,1,0:T(8,128)S(1)}, f32[3,32,128]{2,1,0:T(8,128)S(1)}, u32[]{:S(2)}, u32[]{:S(2)}) collective-permute-start(f32[3,32,128]{2,1,0:T(8,128)S(1)} %get-tuple-element.53), channel_id=1, source_target_pairs={{16,0},{32,16},{48,32},{64,48},{80,64},{96,80},{112,96},{128,112},... | collective-permute-start | bytes 147464 | tf_op jit(solution)/shard_map/ppermute | solution.py:19
  107.1 12.0 %collective-permute-start.12 = (f32[3,32,128]{2,1,0:T(8,128)S(1)}, f32[3,32,128]{2,1,0:T(8,128)S(1)}, u32[]{:S(2)}, u32[]{:S(2)}) collective-permute-start(f32[3,32,128]{2,1,0:T(8,128)S(1)} %get-tuple-element.52), channel_id=1, source_target_pairs={{0,16},{16,32},{32,48},{48,64},{64,80},{80,96},{96,112},{112,128},... | collective-permute-start | bytes 147464 | tf_op jit(solution)/shard_map/ppermute | solution.py:18
  119.1 6.5 %collective-permute-start.15 = (f32[38,3,128]{2,1,0:T(4,128)S(1)}, f32[38,3,128]{2,1,0:T(4,128)S(1)}, u32[]{:S(2)}, u32[]{:S(2)}) collective-permute-start(f32[38,3,128]{2,1,0:T(4,128)S(1)} %get-tuple-element.45), channel_id=1, source_target_pairs={{4,0},{8,4},{12,8},{0,12},{5,1},{9,5},{13,9},{1,13},{6,2},{10,6},{... | collective-permute-start | bytes 175112 | tf_op jit(solution)/shard_map/ppermute | solution.py:19
  121.1 7.5 %collective-permute-start.14 = (f32[38,3,128]{2,1,0:T(4,128)S(1)}, f32[38,3,128]{2,1,0:T(4,128)S(1)}, u32[]{:S(2)}, u32[]{:S(2)}) collective-permute-start(f32[38,3,128]{2,1,0:T(4,128)S(1)} %get-tuple-element.44), channel_id=1, source_target_pairs={{0,4},{4,8},{8,12},{12,0},{1,5},{5,9},{9,13},{13,1},{2,6},{6,10},{... | collective-permute-start | bytes 175112 | tf_op jit(solution)/shard_map/ppermute | solution.py:18
  129.3 6.5 %collective-permute-start.16 = (f32[38,38,3]{1,0,2:T(8,128)S(1)}, f32[38,38,3]{1,0,2:T(8,128)S(1)}, u32[]{:S(2)}, u32[]{:S(2)}) collective-permute-start(f32[38,38,3]{1,0,2:T(8,128)S(1)} %copy.18), channel_id=1, source_target_pairs={{0,1},{1,2},{2,3},{3,0},{4,5},{5,6},{6,7},{7,4},{8,9},{9,10},{10,1... | collective-permute-start | bytes 51992 | tf_op jit(solution)/shard_map/ppermute | solution.py:18
  133.6 6.1 %collective-permute-start.17 = (f32[38,38,3]{1,0,2:T(8,128)S(1)}, f32[38,38,3]{1,0,2:T(8,128)S(1)}, u32[]{:S(2)}, u32[]{:S(2)}) collective-permute-start(f32[38,38,3]{1,0,2:T(8,128)S(1)} %copy.20), channel_id=1, source_target_pairs={{1,0},{2,1},{3,2},{0,3},{5,4},{6,5},{7,6},{4,7},{9,8},{10,9},{11,1... | collective-permute-start | bytes 51992 | tf_op jit(solution)/shard_map/ppermute | solution.py:19
  141.0 2.2 %copy-start.3 = (bf16[3,32,32,128]{3,2,1,0:T(8,128)(2,1)S(1)}, bf16[3,32,32,128]{3,2,1,0:T(8,128)(2,1)}, u32[]{:S(2)}) copy-start(bf16[3,32,32,128]{3,2,1,0:T(8,128)(2,1)} %param.5) | copy-start | bytes 2359300
  143.2 28.2 %copy-start.4 = (s32[4]{0:T(128)S(1)}, s32[4]{0:T(128)}, u32[]{:S(2)}) copy-start(s32[4]{0:T(128)} %param.7) | copy-start | bytes 52
  152.6 4.3 %collective-permute-start.19 = (bf16[1,32,128]{2,1,0:T(8,128)(2,1)S(1)}, bf16[1,32,128]{2,1,0:T(8,128)(2,1)S(1)}, u32[]{:S(2)}, u32[]{:S(2)}) collective-permute-start(bf16[1,32,128]{2,1,0:T(8,128)(2,1)S(1)} %get-tuple-element.64), channel_id=1, source_target_pairs={{16,0},{32,16},{48,32},{64,48},{80,64},{96,80},{112,96},{128,112},... | collective-permute-start | bytes 24584 | tf_op jit(solution)/shard_map/ppermute | solution.py:19
  154.5 11.0 %collective-permute-start.18 = (bf16[1,32,128]{2,1,0:T(8,128)(2,1)S(1)}, bf16[1,32,128]{2,1,0:T(8,128)(2,1)S(1)}, u32[]{:S(2)}, u32[]{:S(2)}) collective-permute-start(bf16[1,32,128]{2,1,0:T(8,128)(2,1)S(1)} %get-tuple-element.63), channel_id=1, source_target_pairs={{0,16},{16,32},{32,48},{48,64},{64,80},{80,96},{96,112},{112,128},... | collective-permute-start | bytes 24584 | tf_op jit(solution)/shard_map/ppermute | solution.py:18
  165.5 7.7 %collective-permute-start.21 = (bf16[34,1,128]{2,1,0:T(2,128)(2,1)S(1)}, bf16[34,1,128]{2,1,0:T(2,128)(2,1)S(1)}, u32[]{:S(2)}, u32[]{:S(2)}) collective-permute-start(bf16[34,1,128]{2,1,0:T(2,128)(2,1)S(1)} %get-tuple-element.62), channel_id=1, source_target_pairs={{4,0},{8,4},{12,8},{0,12},{5,1},{9,5},{13,9},{1,13},{6,2},{10,6},{... | collective-permute-start | bytes 26120 | tf_op jit(solution)/shard_map/ppermute | solution.py:19
  167.7 6.9 %collective-permute-start.20 = (bf16[34,1,128]{2,1,0:T(2,128)(2,1)S(1)}, bf16[34,1,128]{2,1,0:T(2,128)(2,1)S(1)}, u32[]{:S(2)}, u32[]{:S(2)}) collective-permute-start(bf16[34,1,128]{2,1,0:T(2,128)(2,1)S(1)} %get-tuple-element.61), channel_id=1, source_target_pairs={{0,4},{4,8},{8,12},{12,0},{1,5},{5,9},{9,13},{13,1},{2,6},{6,10},{... | collective-permute-start | bytes 26120 | tf_op jit(solution)/shard_map/ppermute | solution.py:18
  (3 other events, 6.1 us)
